TPU v7x, 512 devices: a whole 4x4x16 slice. The times are simulated.
512 devices in a mesh: cluster: 128 (over z, y, x_lo), feat: 4 (over x_hi, core).
Axes of the slice: x: 4 (x_hi: 2, x_lo: 2; x = x_hi * 2 + x_lo), y: 4, z: 16, core: 2. Of those that a mesh axis runs over, the one named last changes fastest.
Arguments:
- queries: bfloat16 [32768, 1024], P('cluster', 'feat'), may hold values from -6 to 6
- assign: int32 [32768, 1], P('cluster'), may hold values from 0 to 127, as said below
- band_mask: int32 [128, 7], replicated, may hold values from 0 to 1, as said below
- keys: bfloat16 [65536, 1024], P(('cluster', 'feat')), may hold values from -6 to 6
- labels: bfloat16 [65536, 1000], P(('cluster', 'feat')), may hold values from -24 to 24
- prior: bfloat16 [65536], P(('cluster', 'feat')), may hold values from -2 to 506
Outputs:
- propagated: bfloat16 [32768, 1000], P('cluster', 'feat')
Inputs may be any that keep to these rules, and one draw needn't show every extreme that they name: `assign`: in each aligned block of 256 rows at most 4 rows name one cluster. `band_mask`: entry 3 of every row is 1.
All inputs are finite; a program needn't handle non-finite values.
Results may differ from a plain program's by a relative error of at most 0.014.
Values may be sent and summed in bfloat16 or wider, within the bound.
No kernel may reach another device: no remote copies, remote signals or barrier semaphores. Data moves between devices by JAX's collectives and lax.ppermute only.
A program may use at most 64 MiB of HBM per device.

v0:
```python
import math
import jax
import jax.numpy as jnp
from jax import lax
from jax.sharding import Mesh
from jax.sharding import PartitionSpec as P

REACH = 3
temper = 2.0
CLUSTER = ("outer", "inner")


def routed(array, forward):
    outer = lax.axis_size("outer")
    inner = lax.axis_size("inner")
    tail = array.shape[1:]
    grid = array.reshape((outer, inner) + tail)
    stages = ("inner", "outer") if forward else ("outer", "inner")
    for axis in stages:
        if axis == "inner":
            grid = jnp.swapaxes(grid, 0, 1)
        grid = lax.all_to_all(grid, axis, split_axis=0, concat_axis=0, tiled=True)
        if axis == "inner":
            grid = jnp.swapaxes(grid, 0, 1)
    return grid.reshape(array.shape)


def shifted(array, axis, by):
    peers = lax.axis_size(axis)
    return lax.ppermute(array, axis, [(i, (i - by) % peers) for i in range(peers)])


def swapped(array, axis, bit):
    peers = lax.axis_size(axis)
    return lax.ppermute(array, axis, [(i, i ^ bit) for i in range(peers)])


def round_bf16(x):
    return lax.reduce_precision(x, exponent_bits=8, mantissa_bits=7)


def split3(x):
    hi = round_bf16(x)
    rest = x - hi
    mid = round_bf16(rest)
    lo = rest - mid
    return [part.astype(jnp.bfloat16) for part in (hi, mid, lo)]


def join3(parts):
    hi, mid, lo = [p.astype(jnp.float32) for p in parts]
    return hi + mid + lo


def pack(part, top, total, width):
    rows = part.shape[0]
    codes = split3(top) + split3(total)
    columns = [part.astype(jnp.bfloat16)] + [c[:, None] for c in codes]
    pad = width - part.shape[1] - len(codes)
    columns.append(jnp.zeros((rows, pad), jnp.bfloat16))
    return jnp.concatenate(columns, axis=1)


def merge(kept, top, total, message, width):
    other = message[:, :width].astype(jnp.float32)
    codes = [message[:, width + i] for i in range(6)]
    other_top = join3(codes[:3])
    other_total = join3(codes[3:])
    highest = jnp.maximum(top, other_top)
    mine = jnp.exp(top - highest)
    theirs = jnp.exp(other_top - highest)
    merged = kept * mine[:, None] + other * theirs[:, None]
    return (merged, highest, total * mine + other_total * theirs)


def body(queries, assign, band_mask, keys, labels, prior):
    clusters = lax.axis_size(CLUSTER)
    cluster_index = lax.axis_index(CLUSTER)
    feat_index = lax.axis_index("feat")
    local_rows = queries.shape[0]
    depth = keys.shape[1]
    classes = labels.shape[1]
    rows = keys.shape[0]
    capacity = 2 * local_rows // clusters
    slots = clusters * capacity
    width = depth + classes + 1
    padded = -(-width // 128) * 128
    block = jnp.concatenate(
        [keys, labels, prior[:, None], jnp.zeros((rows, padded - width), keys.dtype)], axis=1
    )
    offsets = [0]
    for reach in range(1, REACH + 1):
        offsets += [reach, -reach]
    blocks = [block] + [shifted(block, CLUSTER, o) for o in offsets[1:]]
    target = assign[:, 0]
    onehot = (target[:, None] == jnp.arange(clusters, dtype=jnp.int32)[None, :]).astype(jnp.int32)
    before = jnp.cumsum(onehot, axis=0) - onehot
    position = target * capacity + jnp.sum(before * onehot, axis=1)
    outgoing = jnp.zeros((slots, queries.shape[1]), queries.dtype).at[position].set(queries)
    arrived = routed(outgoing.reshape(clusters, capacity, queries.shape[1]), True)
    query_full = lax.all_gather(
        arrived.reshape(slots, queries.shape[1]), "feat", axis=1, tiled=True
    )
    stacked = jnp.stack(blocks)
    band_keys = stacked[:, :, :depth].reshape(len(offsets) * rows, depth)
    band_labels = stacked[:, :, depth : depth + classes].reshape(len(offsets) * rows, classes)
    band_prior = stacked[:, :, depth + classes].reshape(len(offsets) * rows)
    mask_row = band_mask[cluster_index]
    live_blocks = jnp.stack([mask_row[REACH + o] > 0 for o in offsets])
    live = jnp.repeat(live_blocks, rows)
    scale = temper / math.sqrt(depth)
    scores = (
        jnp.einsum("qd,kd->qk", query_full, band_keys, preferred_element_type=jnp.float32) * scale
    )
    scores = scores + band_prior.astype(jnp.float32)[None, :]
    scores = jnp.where(live[None, :], scores, -jnp.inf)
    top = jnp.max(scores, axis=1)
    weight = jnp.exp(scores - top[:, None])
    total = jnp.sum(weight, axis=1)
    accum = jnp.dot(weight.astype(jnp.bfloat16), band_labels, preferred_element_type=jnp.float32)
    quarter = classes // 4
    core = feat_index % 2
    side = feat_index // 2
    grid = accum.reshape(slots, 2, 2, quarter)
    kept = lax.dynamic_index_in_dim(grid, core, axis=2, keepdims=False)
    sent = lax.dynamic_index_in_dim(grid, 1 - core, axis=2, keepdims=False)
    message = swapped(
        pack(sent.reshape(slots, 2 * quarter), top, total, 2 * quarter + 12), "feat", 1
    )
    kept, top, total = merge(kept.reshape(slots, 2 * quarter), top, total, message, 2 * quarter)
    grid = kept.reshape(slots, 2, quarter)
    kept = lax.dynamic_index_in_dim(grid, side, axis=1, keepdims=False)
    sent = lax.dynamic_index_in_dim(grid, 1 - side, axis=1, keepdims=False)
    message = swapped(pack(sent, top, total, quarter + 6), "feat", 2)
    kept, top, total = merge(kept, top, total, message, quarter)
    shares = (kept / total[:, None]).astype(jnp.bfloat16)
    returned = routed(shares.reshape(clusters, capacity, quarter), False)
    return returned.reshape(slots, quarter)[position]


def solution(mesh):
    clusters = mesh.shape["cluster"]
    inner = 8 if clusters % 8 == 0 else 1
    split = Mesh(
        mesh.devices.reshape(clusters // inner, inner, mesh.shape["feat"]),
        ("outer", "inner", "feat"),
    )
    in_specs = (
        P(CLUSTER, "feat"),
        P(CLUSTER, None),
        P(),
        P(CLUSTER + ("feat",), None),
        P(CLUSTER + ("feat",), None),
        P(CLUSTER + ("feat",)),
    )
    out_specs = P(CLUSTER, "feat")
    return jax.shard_map(body, mesh=split, in_specs=in_specs, out_specs=out_specs, check_vma=False)
```

profile of v0, /device:TPU:64, one launch (start us, length us, event | category | flops | bytes accessed | tf_op | source)
XLA Modules:
  0.0 194.4 jit_solution(8708139541104495941)
XLA Ops:
  9.6 5.4 %collective-permute-start = (bf16[128,2048]{1,0:T(8,128)(2,1)S(1)}, bf16[128,2048]{1,0:T(8,128)(2,1)}, u32[]{:S(2)}, u32[]{:S(2)}) collective-permute-start(bf16[128,2048]{1,0:T(8,128)(2,1)S(1)} %concatenate.9), channel_id=1, source_target_pairs={{0,508},{4,0},{8,4},{12,8},{16,12},{20,16},{24,20},{28,24},{32,28}... | collective-permute-start | bytes 1572872 | tf_op jit(solution)/shard_map/ppermute | solution.py:30
  15.0 1.9 collective-permute-start.1
  16.9 3.0 %collective-permute-start.2 = (bf16[128,2048]{1,0:T(8,128)(2,1)S(1)}, bf16[128,2048]{1,0:T(8,128)(2,1)S(1)}, u32[]{:S(2)}, u32[]{:S(2)}) collective-permute-start(bf16[128,2048]{1,0:T(8,128)(2,1)S(1)} %concatenate.9), channel_id=1, source_target_pairs={{0,504},{4,508},{8,0},{12,4},{16,8},{20,12},{24,16},{28,20},{32,24... | collective-permute-start | bytes 1572872 | tf_op jit(solution)/shard_map/ppermute | solution.py:30
  19.9 2.8 %collective-permute-start.3 = (bf16[128,2048]{1,0:T(8,128)(2,1)S(1)}, bf16[128,2048]{1,0:T(8,128)(2,1)S(1)}, u32[]{:S(2)}, u32[]{:S(2)}) collective-permute-start(bf16[128,2048]{1,0:T(8,128)(2,1)S(1)} %concatenate.9), channel_id=1, source_target_pairs={{0,8},{4,12},{8,16},{12,20},{16,24},{20,28},{24,32},{28,36},{32,40... | collective-permute-start | bytes 1572872 | tf_op jit(solution)/shard_map/ppermute | solution.py:30
  22.8 6.4 %collective-permute-start.4 = (bf16[128,2048]{1,0:T(8,128)(2,1)S(1)}, bf16[128,2048]{1,0:T(8,128)(2,1)S(1)}, u32[]{:S(2)}, u32[]{:S(2)}) collective-permute-start(bf16[128,2048]{1,0:T(8,128)(2,1)S(1)} %concatenate.9), channel_id=1, source_target_pairs={{0,500},{4,504},{8,508},{12,0},{16,4},{20,8},{24,12},{28,16},{32,2... | collective-permute-start | bytes 1572872 | tf_op jit(solution)/shard_map/ppermute | solution.py:30
  30.5 1.9 scatter_custom_fusion
  33.3 4.8 %all-to-all-start = ((bf16[8,16,4,256]{3,2,1,0:T(4,128)(2,1)}), bf16[8,16,4,256]{3,2,1,0:T(4,128)(2,1)S(1)}, u32[]{:S(2)}, u32[]{:S(2)}) async-start(bf16[8,16,4,256]{3,2,1,0:T(4,128)(2,1)} %bitcast.80), calls=%async_computation | async-start | bytes 524288 | tf_op jit(solution)/shard_map/all_to_all | solution.py:22
  44.0 8.9 %all-to-all-done = bf16[8,16,4,256]{3,2,1,0:T(4,128)(2,1)S(1)} async-done(((bf16[8,16,4,256]{3,2,1,0:T(4,128)(2,1)}), bf16[8,16,4,256]{3,2,1,0:T(4,128)(2,1)S(1)}, u32[]{:S(2)}, u32[]{:S(2)}) %all-to-all-start) | async-done | bytes 262176 | tf_op jit(solution)/shard_map/all_to_all | solution.py:22
  53.8 14.9 %all-to-all-start.1 = ((bf16[16,8,4,256]{3,2,1,0:T(4,128)(2,1)}), bf16[16,8,4,256]{3,2,1,0:T(4,128)(2,1)S(1)}, u32[]{:S(2)}, u32[]{:S(2)}) async-start(bf16[16,8,4,256]{3,2,1,0:T(4,128)(2,1)} %copy.50), calls=%async_computation.1 | async-start | bytes 524288 | tf_op jit(solution)/shard_map/all_to_all | solution.py:22
  68.8 11.5 %collective-permute-start.5 = (bf16[128,2048]{1,0:T(8,128)(2,1)S(1)}, bf16[128,2048]{1,0:T(8,128)(2,1)}, u32[]{:S(2)}, u32[]{:S(2)}) collective-permute-start(bf16[128,2048]{1,0:T(8,128)(2,1)S(1)} %concatenate.9), channel_id=1, source_target_pairs={{0,12},{4,16},{8,20},{12,24},{16,28},{20,32},{24,36},{28,40},{32,4... | collective-permute-start | bytes 1572872 | tf_op jit(solution)/shard_map/ppermute | solution.py:30
  80.3 1.9 bitcast_dynamic-update-slice_fusion.5
  83.0 3.7 %all-to-all-done.1 = bf16[16,8,4,256]{3,2,1,0:T(4,128)(2,1)S(1)} async-done(((bf16[16,8,4,256]{3,2,1,0:T(4,128)(2,1)}), bf16[16,8,4,256]{3,2,1,0:T(4,128)(2,1)S(1)}, u32[]{:S(2)}, u32[]{:S(2)}) %all-to-all-start.1) | async-done | bytes 262176 | tf_op jit(solution)/shard_map/all_to_all | solution.py:22
  90.1 11.3 %collective-permute-done.5 = bf16[128,2048]{1,0:T(8,128)(2,1)} collective-permute-done((bf16[128,2048]{1,0:T(8,128)(2,1)S(1)}, bf16[128,2048]{1,0:T(8,128)(2,1)}, u32[]{:S(2)}, u32[]{:S(2)}) %collective-permute-start.5) | collective-permute-done | bytes 524320 | tf_op jit(solution)/shard_map/ppermute | solution.py:30
  101.3 1.9 bitcast_dynamic-update-slice_fusion
  103.2 1.8 slice.116
  107.3 3.0 %reshape.184 = bf16[2,2,250,896]{2,1,0,3:T(2,128)(2,1)} reshape(bf16[1000,896]{0,1:T(8,128)(2,1)S(1)} %bitcast.84) | data formatting | bytes 3584000 | tf_op jit(solution)/shard_map/dot_general | solution.py:120
  111.4 6.3 %all-gather.2.cloned.1.call-done = bf16[512,1024]{1,0:T(8,128)(2,1)} async-done(((bf16[512,256]{1,0:T(8,128)(2,1)}), bf16[512,1024]{1,0:T(8,128)(2,1)}) %all-gather.2.cloned.1.call-update) | async-done | bytes 1048592 | tf_op jit(solution)/shard_map/all_gather | solution.py:101
  117.7 3.2 %fusion.40 = (f32[512]{0:T(512)S(1)}, f32[512,896]{1,0:T(8,128)S(1)}) fusion(f32[896]{0:T(1024)S(1)} %bitcast.103, bf16[512,1024]{1,0:T(8,128)(2,1)} %all-gather.2.cloned.1.call-done, bf16[896,1024]{1,0:T(8,128)(2,1)} %bitcast.85, pred[896]{0:T(1024)(128)(4,1)S(1)} %broadcast_bitcast_fusion), kind=kOutput, calls=%fused_computation.95 | convolution fusion | flops 941358592 | bytes 4725120 | tf_op jit(solution)/shard_map/qd,kd->qk/dot_general | solution.py:113
  125.7 2.2 %collective-permute-start.6 = (bf16[512,512]{0,1:T(8,128)(2,1)S(1)}, bf16[512,512]{0,1:T(8,128)(2,1)S(1)}, u32[]{:S(2)}, u32[]{:S(2)}) collective-permute-start(bf16[512,512]{0,1:T(8,128)(2,1)S(1)} %concatenate.10), channel_id=1, source_target_pairs={{0,1},{1,0},{2,3},{3,2},{4,5},{5,4},{6,7},{7,6},{8,9},{9,8},{10,11... | collective-permute-start | bytes 1572872 | tf_op jit(solution)/shard_map/ppermute | solution.py:35
  130.1 2.5 %collective-permute-start.7 = (bf16[512,256]{0,1:T(8,128)(2,1)S(1)}, bf16[512,256]{0,1:T(8,128)(2,1)S(1)}, u32[]{:S(2)}, u32[]{:S(2)}) collective-permute-start(bf16[512,256]{0,1:T(8,128)(2,1)S(1)} %concatenate.11), channel_id=1, source_target_pairs={{0,2},{1,3},{2,0},{3,1},{4,6},{5,7},{6,4},{7,5},{8,10},{9,11},{10,... | collective-permute-start | bytes 786440 | tf_op jit(solution)/shard_map/ppermute | solution.py:35
  132.6 9.4 %collective-permute-done.7 = bf16[512,256]{0,1:T(8,128)(2,1)S(1)} collective-permute-done((bf16[512,256]{0,1:T(8,128)(2,1)S(1)}, bf16[512,256]{0,1:T(8,128)(2,1)S(1)}, u32[]{:S(2)}, u32[]{:S(2)}) %collective-permute-start.7) | collective-permute-done | bytes 262176 | tf_op jit(solution)/shard_map/ppermute | solution.py:35
  142.3 30.7 %all_to_all.20 = bf16[16,8,4,250]{3,2,1,0:T(4,128)(2,1)S(1)} all-to-all(bf16[16,8,4,250]{3,2,1,0:T(4,128)(2,1)S(1)} %reshape_reshape.14), channel_id=1, replica_groups=mesh['outer'=16,'inner'=8,'feat'=4] {'outer'}, dimensions={0} | all-to-all | bytes 512000 | tf_op jit(solution)/shard_map/all_to_all | solution.py:22
  173.8 4.3 %all-to-all-start.3 = ((bf16[8,16,4,250]{3,2,1,0:T(4,128)(2,1)}), bf16[8,16,4,250]{3,2,1,0:T(4,128)(2,1)S(1)}, u32[]{:S(2)}, u32[]{:S(2)}) async-start(bf16[8,16,4,250]{3,2,1,0:T(4,128)(2,1)} %copy.55), calls=%async_computation.3 | async-start | bytes 524288 | tf_op jit(solution)/shard_map/all_to_all | solution.py:22
  178.1 7.3 %all-to-all-done.3 = bf16[8,16,4,250]{3,2,1,0:T(4,128)(2,1)S(1)} async-done(((bf16[8,16,4,250]{3,2,1,0:T(4,128)(2,1)}), bf16[8,16,4,250]{3,2,1,0:T(4,128)(2,1)S(1)}, u32[]{:S(2)}, u32[]{:S(2)}) %all-to-all-start.3) | async-done | bytes 256032 | tf_op jit(solution)/shard_map/all_to_all | solution.py:22
  (72 shorter events, 25.4 us)
Async XLA Ops:
  6.5 32.4 %copy-start = (s32[128,7]{0,1:T(8,128)S(1)}, s32[128,7]{0,1:T(8,128)}, u32[]{:S(2)}) copy-start(s32[128,7]{0,1:T(8,128)} %param.8) | copy-start | bytes 10756
  6.5 23.7 %copy-start.4 = (s32[256,1]{0,1:T(1,128)S(1)}, s32[256,1]{0,1:T(1,128)}, u32[]{:S(2)}) copy-start(s32[256,1]{0,1:T(1,128)} %param.7) | copy-start | bytes 3076
  9.6 59.2 %collective-permute-start = (bf16[128,2048]{1,0:T(8,128)(2,1)S(1)}, bf16[128,2048]{1,0:T(8,128)(2,1)}, u32[]{:S(2)}, u32[]{:S(2)}) collective-permute-start(bf16[128,2048]{1,0:T(8,128)(2,1)S(1)} %concatenate.9), channel_id=1, source_target_pairs={{0,508},{4,0},{8,4},{12,8},{16,12},{20,16},{24,20},{28,24},{32,28}... | collective-permute-start | bytes 1572872 | tf_op jit(solution)/shard_map/ppermute | solution.py:30
  15.0 67.1 %collective-permute-start.1 = (bf16[128,2048]{1,0:T(8,128)(2,1)S(1)}, bf16[128,2048]{1,0:T(8,128)(2,1)S(1)}, u32[]{:S(2)}, u32[]{:S(2)}) collective-permute-start(bf16[128,2048]{1,0:T(8,128)(2,1)S(1)} %concatenate.9), channel_id=1, source_target_pairs={{0,4},{4,8},{8,12},{12,16},{16,20},{20,24},{24,28},{28,32},{32,36}... | collective-permute-start | bytes 1572872 | tf_op jit(solution)/shard_map/ppermute | solution.py:30
  16.9 70.6 %collective-permute-start.2 = (bf16[128,2048]{1,0:T(8,128)(2,1)S(1)}, bf16[128,2048]{1,0:T(8,128)(2,1)S(1)}, u32[]{:S(2)}, u32[]{:S(2)}) collective-permute-start(bf16[128,2048]{1,0:T(8,128)(2,1)S(1)} %concatenate.9), channel_id=1, source_target_pairs={{0,504},{4,508},{8,0},{12,4},{16,8},{20,12},{24,16},{28,20},{32,24... | collective-permute-start | bytes 1572872 | tf_op jit(solution)/shard_map/ppermute | solution.py:30
  19.9 68.4 %collective-permute-start.3 = (bf16[128,2048]{1,0:T(8,128)(2,1)S(1)}, bf16[128,2048]{1,0:T(8,128)(2,1)S(1)}, u32[]{:S(2)}, u32[]{:S(2)}) collective-permute-start(bf16[128,2048]{1,0:T(8,128)(2,1)S(1)} %concatenate.9), channel_id=1, source_target_pairs={{0,8},{4,12},{8,16},{12,20},{16,24},{20,28},{24,32},{28,36},{32,40... | collective-permute-start | bytes 1572872 | tf_op jit(solution)/shard_map/ppermute | solution.py:30
  22.8 66.4 %collective-permute-start.4 = (bf16[128,2048]{1,0:T(8,128)(2,1)S(1)}, bf16[128,2048]{1,0:T(8,128)(2,1)S(1)}, u32[]{:S(2)}, u32[]{:S(2)}) collective-permute-start(bf16[128,2048]{1,0:T(8,128)(2,1)S(1)} %concatenate.9), channel_id=1, source_target_pairs={{0,500},{4,504},{8,508},{12,0},{16,4},{20,8},{24,12},{28,16},{32,2... | collective-permute-start | bytes 1572872 | tf_op jit(solution)/shard_map/ppermute | solution.py:30
  33.3 19.7 %all-to-all-start = ((bf16[8,16,4,256]{3,2,1,0:T(4,128)(2,1)}), bf16[8,16,4,256]{3,2,1,0:T(4,128)(2,1)S(1)}, u32[]{:S(2)}, u32[]{:S(2)}) async-start(bf16[8,16,4,256]{3,2,1,0:T(4,128)(2,1)} %bitcast.80), calls=%async_computation | async-start | bytes 524288 | tf_op jit(solution)/shard_map/all_to_all | solution.py:22
  53.8 33.0 %all-to-all-start.1 = ((bf16[16,8,4,256]{3,2,1,0:T(4,128)(2,1)}), bf16[16,8,4,256]{3,2,1,0:T(4,128)(2,1)S(1)}, u32[]{:S(2)}, u32[]{:S(2)}) async-start(bf16[16,8,4,256]{3,2,1,0:T(4,128)(2,1)} %copy.50), calls=%async_computation.1 | async-start | bytes 524288 | tf_op jit(solution)/shard_map/all_to_all | solution.py:22
  68.7 49.0 %all-gather.2.cloned.1.call-start = ((), (), s32[]{:S(2)}) async-start(), calls=%async_computation.4 | async-start | bytes 1310720 | tf_op jit(solution)/shard_map/all_gather | solution.py:101
  68.8 32.6 %collective-permute-start.5 = (bf16[128,2048]{1,0:T(8,128)(2,1)S(1)}, bf16[128,2048]{1,0:T(8,128)(2,1)}, u32[]{:S(2)}, u32[]{:S(2)}) collective-permute-start(bf16[128,2048]{1,0:T(8,128)(2,1)S(1)} %concatenate.9), channel_id=1, source_target_pairs={{0,12},{4,16},{8,20},{12,24},{16,28},{20,32},{24,36},{28,40},{32,4... | collective-permute-start | bytes 1572872 | tf_op jit(solution)/shard_map/ppermute | solution.py:30
  103.2 2.6 %copy-start.1 = (bf16[7,128,2048]{2,1,0:T(8,128)(2,1)S(1)}, bf16[7,128,2048]{2,1,0:T(8,128)(2,1)}, u32[]{:S(2)}) copy-start(bf16[7,128,2048]{2,1,0:T(8,128)(2,1)} %bitcast_dynamic-update-slice_fusion) | copy-start | bytes 11010052
  120.9 1.5 copy-start.2
  123.8 1.3 copy-start.3
  125.7 3.8 %collective-permute-start.6 = (bf16[512,512]{0,1:T(8,128)(2,1)S(1)}, bf16[512,512]{0,1:T(8,128)(2,1)S(1)}, u32[]{:S(2)}, u32[]{:S(2)}) collective-permute-start(bf16[512,512]{0,1:T(8,128)(2,1)S(1)} %concatenate.10), channel_id=1, source_target_pairs={{0,1},{1,0},{2,3},{3,2},{4,5},{5,4},{6,7},{7,6},{8,9},{9,8},{10,11... | collective-permute-start | bytes 1572872 | tf_op jit(solution)/shard_map/ppermute | solution.py:35
  130.1 11.9 %collective-permute-start.7 = (bf16[512,256]{0,1:T(8,128)(2,1)S(1)}, bf16[512,256]{0,1:T(8,128)(2,1)S(1)}, u32[]{:S(2)}, u32[]{:S(2)}) collective-permute-start(bf16[512,256]{0,1:T(8,128)(2,1)S(1)} %concatenate.11), channel_id=1, source_target_pairs={{0,2},{1,3},{2,0},{3,1},{4,6},{5,7},{6,4},{7,5},{8,10},{9,11},{10,... | collective-permute-start | bytes 786440 | tf_op jit(solution)/shard_map/ppermute | solution.py:35
  173.8 11.6 %all-to-all-start.3 = ((bf16[8,16,4,250]{3,2,1,0:T(4,128)(2,1)}), bf16[8,16,4,250]{3,2,1,0:T(4,128)(2,1)S(1)}, u32[]{:S(2)}, u32[]{:S(2)}) async-start(bf16[8,16,4,250]{3,2,1,0:T(4,128)(2,1)} %copy.55), calls=%async_computation.3 | async-start | bytes 524288 | tf_op jit(solution)/shard_map/all_to_all | solution.py:22
Sparse Core Ops, SparseCore 0:
  87.7 29.9 all-gather.1
where the time goes:
time: 195 us; the launch traced here: 194 us
  starting transfers between devices  59.6 us (31%)
  waiting for transfers between devices  47.1 us (24%)
  local copies, waits for them, and re-layouts  31.7 us (16%)
  blocking collectives  30.7 us (16%)
  between operations  18.1 us (9%)
  matrix products  4.64 us (2%)
  other arithmetic  2.49 us (1%)
    ppermute x6, starting transfers between devices, shifted(): lax.ppermute(array, axis, [(i, (i - by) % peers) for i in range(peers)])  31 us
    all_to_all x1, blocking collectives, routed(): grid = lax.all_to_all(grid, axis, split_axis=0, concat_axis=0, tiled=True)  30.7 us
    all_to_all x3, starting transfers between devices, routed(): grid = lax.all_to_all(grid, axis, split_axis=0, concat_axis=0, tiled=True)  24 us
    all_to_all x3, waiting for transfers between devices, routed(): grid = lax.all_to_all(grid, axis, split_axis=0, concat_axis=0, tiled=True)  19.9 us
    ppermute x6, waiting for transfers between devices, shifted(): lax.ppermute(array, axis, [(i, (i - by) % peers) for i in range(peers)])  11.3 us
    unnamed x18, local copies, waits for them, and re-layouts  10.4 us
    ppermute x2, waiting for transfers between devices, swapped(): return lax.ppermute(array, axis, [(i, i ^ bit) for i in range(peers)])  9.58 us
    all_gather x1, waiting for transfers between devices, body(): lax.all_gather(arrived.reshape(slots, queries.shape[1]), 'feat', axis=1,...  6.28 us
  transfers between devices with their start and end apart: 12, of which 7 were waited for; matrix products, arithmetic and copies ran while one was open for 12% of the time, Pallas kernels for 0%

commit v1 on v0

--- a/solution.py
+++ b/solution.py
@@ -1,3 +1,4 @@
+import functools
 import math
 import jax
 import jax.numpy as jnp
@@ -8,6 +9,18 @@
 REACH = 3
 temper = 2.0
 CLUSTER = ("outer", "inner")
+
+
+def arrange_bands(patch, lane_axis):
+    runs = []
+    for _ in range(lax.psum(1, lane_axis)):
+        runs.append(patch)
+    val = jnp.stack(runs)
+    f_now = lax.all_to_all(val, lane_axis, 0, 0)
+    return jnp.concatenate(f_now, 1)
+
+
+body_divide = functools.partial(arrange_bands, lane_axis="feat")
 
 
 def routed(array, forward):
@@ -98,9 +111,7 @@
     position = target * capacity + jnp.sum(before * onehot, axis=1)
     outgoing = jnp.zeros((slots, queries.shape[1]), queries.dtype).at[position].set(queries)
     arrived = routed(outgoing.reshape(clusters, capacity, queries.shape[1]), True)
-    query_full = lax.all_gather(
-        arrived.reshape(slots, queries.shape[1]), "feat", axis=1, tiled=True
-    )
+    query_full = body_divide(arrived.reshape(slots, queries.shape[1]))
     stacked = jnp.stack(blocks)
     band_keys = stacked[:, :, :depth].reshape(len(offsets) * rows, depth)
     band_labels = stacked[:, :, depth : depth + classes].reshape(len(offsets) * rows, classes)

time: 195 us -> 175 us (0.90)
  between operations: 18.1 us -> 4.76 us
  waiting for transfers between devices: 47.1 us -> 34 us
  starting transfers between devices: 59.6 us -> 65.6 us
    all_gather x1 -> x0, waiting for transfers between devices: 6.28 us -> none  [body(): lax.all_gather(arrived.reshape(slots, queries.shape[1]), 'feat', axis=1,...]
    all_to_all x0 -> x1, starting transfers between devices: none -> 4.47 us  [arrange_bands(): f_now = lax.all_to_all(val, lane_axis, 0, 0)]
    ppermute x6, waiting for transfers between devices: 11.3 us -> 8.01 us  [shifted(): lax.ppermute(array, axis, [(i, (i - by) % peers) for i in range(peers)])]
  transfers between devices with their start and end apart: 12 -> 12, of which waited for: 7 -> 6; matrix products, arithmetic and copies ran while one was open for 12% -> 14% of each run, Pallas kernels for 0% -> 0%
where the time goes in v1:
time: 175 us; the launch traced here: 174 us
  starting transfers between devices  65.6 us (37%)
  waiting for transfers between devices  34 us (19%)
  local copies, waits for them, and re-layouts  32.2 us (18%)
  blocking collectives  30.4 us (17%)
  between operations  4.76 us (3%)
  matrix products  4.35 us (2%)
  other arithmetic  2.49 us (1%)
    ppermute x6, starting transfers between devices, shifted(): lax.ppermute(array, axis, [(i, (i - by) % peers) for i in range(peers)])  31 us
    all_to_all x1, blocking collectives, routed(): grid = lax.all_to_all(grid, axis, split_axis=0, concat_axis=0, tiled=True)  30.4 us
    all_to_all x3, starting transfers between devices, routed(): grid = lax.all_to_all(grid, axis, split_axis=0, concat_axis=0, tiled=True)  23.8 us
    all_to_all x3, waiting for transfers between devices, routed(): grid = lax.all_to_all(grid, axis, split_axis=0, concat_axis=0, tiled=True)  18.2 us
    unnamed x18, local copies, waits for them, and re-layouts  10.3 us
    ppermute x6, waiting for transfers between devices, shifted(): lax.ppermute(array, axis, [(i, (i - by) % peers) for i in range(peers)])  8.01 us
    ppermute x2, waiting for transfers between devices, swapped(): return lax.ppermute(array, axis, [(i, i ^ bit) for i in range(peers)])  7.78 us
    ppermute x2, starting transfers between devices, swapped(): return lax.ppermute(array, axis, [(i, i ^ bit) for i in range(peers)])  6.3 us
  transfers between devices with their start and end apart: 12, of which 6 were waited for; matrix products, arithmetic and copies ran while one was open for 14% of the time, Pallas kernels for 0%

profile of v1, /device:TPU:64, one launch (start us, length us, event | category | flops | bytes accessed | tf_op | source)
XLA Modules:
  0.0 173.8 jit_solution(5428680603433696129)
XLA Ops:
  3.1 5.4 %collective-permute-start = (bf16[128,2048]{1,0:T(8,128)(2,1)S(1)}, bf16[128,2048]{1,0:T(8,128)(2,1)}, u32[]{:S(2)}, u32[]{:S(2)}) collective-permute-start(bf16[128,2048]{1,0:T(8,128)(2,1)S(1)} %concatenate.9), channel_id=1, source_target_pairs={{0,508},{4,0},{8,4},{12,8},{16,12},{20,16},{24,20},{28,24},{32,28}... | collective-permute-start | bytes 1572872 | tf_op jit(solution)/shard_map/ppermute | solution.py:43
  8.5 1.9 %collective-permute-start.1 = (bf16[128,2048]{1,0:T(8,128)(2,1)S(1)}, bf16[128,2048]{1,0:T(8,128)(2,1)S(1)}, u32[]{:S(2)}, u32[]{:S(2)}) collective-permute-start(bf16[128,2048]{1,0:T(8,128)(2,1)S(1)} %concatenate.9), channel_id=1, source_target_pairs={{0,4},{4,8},{8,12},{12,16},{16,20},{20,24},{24,28},{28,32},{32,36}... | collective-permute-start | bytes 1572872 | tf_op jit(solution)/shard_map/ppermute | solution.py:43
  10.4 3.0 %collective-permute-start.2 = (bf16[128,2048]{1,0:T(8,128)(2,1)S(1)}, bf16[128,2048]{1,0:T(8,128)(2,1)S(1)}, u32[]{:S(2)}, u32[]{:S(2)}) collective-permute-start(bf16[128,2048]{1,0:T(8,128)(2,1)S(1)} %concatenate.9), channel_id=1, source_target_pairs={{0,504},{4,508},{8,0},{12,4},{16,8},{20,12},{24,16},{28,20},{32,24... | collective-permute-start | bytes 1572872 | tf_op jit(solution)/shard_map/ppermute | solution.py:43
  13.4 2.8 %collective-permute-start.3 = (bf16[128,2048]{1,0:T(8,128)(2,1)S(1)}, bf16[128,2048]{1,0:T(8,128)(2,1)S(1)}, u32[]{:S(2)}, u32[]{:S(2)}) collective-permute-start(bf16[128,2048]{1,0:T(8,128)(2,1)S(1)} %concatenate.9), channel_id=1, source_target_pairs={{0,8},{4,12},{8,16},{12,20},{16,24},{20,28},{24,32},{28,36},{32,40... | collective-permute-start | bytes 1572872 | tf_op jit(solution)/shard_map/ppermute | solution.py:43
  16.3 6.4 %collective-permute-start.4 = (bf16[128,2048]{1,0:T(8,128)(2,1)S(1)}, bf16[128,2048]{1,0:T(8,128)(2,1)S(1)}, u32[]{:S(2)}, u32[]{:S(2)}) collective-permute-start(bf16[128,2048]{1,0:T(8,128)(2,1)S(1)} %concatenate.9), channel_id=1, source_target_pairs={{0,500},{4,504},{8,508},{12,0},{16,4},{20,8},{24,12},{28,16},{32,2... | collective-permute-start | bytes 1572872 | tf_op jit(solution)/shard_map/ppermute | solution.py:43
  23.9 1.9 %scatter_custom_fusion = bf16[512,256]{1,0:T(8,128)(2,1)S(1)} fusion(s32[256]{0:T(256)S(1)} %bitcast.109, bf16[256,256]{1,0:T(8,128)(2,1)} %param.6, bf16[]{:T(256)} %constant.76.clone.1), kind=kCustom, calls=%fused_computation.34 | custom fusion | bytes 262656 | tf_op jit(solution)/shard_map/scatter | solution.py:112
  26.7 4.8 %all-to-all-start = ((bf16[8,16,4,256]{3,2,1,0:T(4,128)(2,1)}), bf16[8,16,4,256]{3,2,1,0:T(4,128)(2,1)S(1)}, u32[]{:S(2)}, u32[]{:S(2)}) async-start(bf16[8,16,4,256]{3,2,1,0:T(4,128)(2,1)} %bitcast.83), calls=%async_computation | async-start | bytes 524288 | tf_op jit(solution)/shard_map/all_to_all | solution.py:35
  37.6 8.8 %all-to-all-done = bf16[8,16,4,256]{3,2,1,0:T(4,128)(2,1)S(1)} async-done(((bf16[8,16,4,256]{3,2,1,0:T(4,128)(2,1)}), bf16[8,16,4,256]{3,2,1,0:T(4,128)(2,1)S(1)}, u32[]{:S(2)}, u32[]{:S(2)}) %all-to-all-start) | async-done | bytes 262176 | tf_op jit(solution)/shard_map/all_to_all | solution.py:35
  47.2 14.9 %all-to-all-start.1 = ((bf16[16,8,4,256]{3,2,1,0:T(4,128)(2,1)}), bf16[16,8,4,256]{3,2,1,0:T(4,128)(2,1)S(1)}, u32[]{:S(2)}, u32[]{:S(2)}) async-start(bf16[16,8,4,256]{3,2,1,0:T(4,128)(2,1)} %copy.53), calls=%async_computation.1 | async-start | bytes 524288 | tf_op jit(solution)/shard_map/all_to_all | solution.py:35
  62.1 11.5 %collective-permute-start.5 = (bf16[128,2048]{1,0:T(8,128)(2,1)S(1)}, bf16[128,2048]{1,0:T(8,128)(2,1)}, u32[]{:S(2)}, u32[]{:S(2)}) collective-permute-start(bf16[128,2048]{1,0:T(8,128)(2,1)S(1)} %concatenate.9), channel_id=1, source_target_pairs={{0,12},{4,16},{8,20},{12,24},{16,28},{20,32},{24,36},{28,40},{32,4... | collective-permute-start | bytes 1572872 | tf_op jit(solution)/shard_map/ppermute | solution.py:43
  73.6 1.9 %bitcast_dynamic-update-slice_fusion.5 = bf16[7,128,2048]{2,1,0:T(8,128)(2,1)} fusion(bf16[7,128,2048]{2,1,0:T(8,128)(2,1)} %bitcast_dynamic-update-slice_fusion.6, bf16[128,2048]{1,0:T(8,128)(2,1)} %collective-permute-done), kind=kLoop, calls=%fused_computation.21 | loop fusion | bytes 1048576
  78.1 2.1 %all-to-all-done.1 = bf16[16,8,4,256]{3,2,1,0:T(4,128)(2,1)S(1)} async-done(((bf16[16,8,4,256]{3,2,1,0:T(4,128)(2,1)}), bf16[16,8,4,256]{3,2,1,0:T(4,128)(2,1)S(1)}, u32[]{:S(2)}, u32[]{:S(2)}) %all-to-all-start.1) | async-done | bytes 262176 | tf_op jit(solution)/shard_map/all_to_all | solution.py:35
  81.5 4.5 %all-to-all-start.2 = ((bf16[4,512,256]{1,2,0:T(8,128)(2,1)}), bf16[4,512,256]{1,2,0:T(8,128)(2,1)S(1)}, u32[]{:S(2)}, u32[]{:S(2)}) async-start(bf16[4,512,256]{1,2,0:T(8,128)(2,1)} %stack.59), calls=%async_computation.2 | async-start | bytes 2097152 | tf_op jit(solution)/shard_map/all_to_all | solution.py:19
  86.8 8.0 %collective-permute-done.5 = bf16[128,2048]{1,0:T(8,128)(2,1)} collective-permute-done((bf16[128,2048]{1,0:T(8,128)(2,1)S(1)}, bf16[128,2048]{1,0:T(8,128)(2,1)}, u32[]{:S(2)}, u32[]{:S(2)}) %collective-permute-start.5) | collective-permute-done | bytes 524320 | tf_op jit(solution)/shard_map/ppermute | solution.py:43
  94.8 1.9 %bitcast_dynamic-update-slice_fusion = bf16[7,128,2048]{2,1,0:T(8,128)(2,1)} fusion(bf16[7,128,2048]{2,1,0:T(8,128)(2,1)} %bitcast_dynamic-update-slice_fusion.1, bf16[128,2048]{1,0:T(8,128)(2,1)} %collective-permute-done.5), kind=kLoop, calls=%fused_computation.16 | loop fusion | bytes 1048576 | tf_op jit(solution)/shard_map/stack | solution.py:115
  96.7 1.8 %slice.116 = bf16[7,128,1000]{2,1,0:T(8,128)(2,1)S(1)} slice(bf16[7,128,2048]{2,1,0:T(8,128)(2,1)} %bitcast_dynamic-update-slice_fusion), slice={[0:7], [0:128], [1024:2024]} | slice | bytes 3584000 | tf_op jit(solution)/shard_map/slice | solution.py:117
  100.7 3.0 %reshape.194 = bf16[2,2,250,896]{2,1,0,3:T(2,128)(2,1)} reshape(bf16[1000,896]{0,1:T(8,128)(2,1)S(1)} %bitcast.87) | data formatting | bytes 3584000 | tf_op jit(solution)/shard_map/dot_general | solution.py:131
  104.9 2.9 %fusion.40 = (f32[512]{0:T(512)S(1)}, f32[512,896]{1,0:T(8,128)S(1)}) fusion(f32[896]{0:T(1024)S(1)} %bitcast.107, bf16[512,1024]{0,1:T(8,128)(2,1)S(1)} %bitcast.89, bf16[896,1024]{1,0:T(8,128)(2,1)} %bitcast.88, pred[896]{0:T(1024)(128)(4,1)S(1)} %broadcast_bitcast_fusion), kind=kOutput, calls=%fused_computation.95 | convolution fusion | flops 941358592 | bytes 4725120 | tf_op jit(solution)/shard_map/qd,kd->qk/dot_general | solution.py:124
  112.7 1.9 %collective-permute-start.6 = (bf16[512,512]{0,1:T(8,128)(2,1)S(1)}, bf16[512,512]{0,1:T(8,128)(2,1)S(1)}, u32[]{:S(2)}, u32[]{:S(2)}) collective-permute-start(bf16[512,512]{0,1:T(8,128)(2,1)S(1)} %concatenate.10), channel_id=1, source_target_pairs={{0,1},{1,0},{2,3},{3,2},{4,5},{5,4},{6,7},{7,6},{8,9},{9,8},{10,11... | collective-permute-start | bytes 1572872 | tf_op jit(solution)/shard_map/ppermute | solution.py:48
  117.0 4.4 %collective-permute-start.7 = (bf16[512,256]{0,1:T(8,128)(2,1)S(1)}, bf16[512,256]{0,1:T(8,128)(2,1)S(1)}, u32[]{:S(2)}, u32[]{:S(2)}) collective-permute-start(bf16[512,256]{0,1:T(8,128)(2,1)S(1)} %concatenate.11), channel_id=1, source_target_pairs={{0,2},{1,3},{2,0},{3,1},{4,6},{5,7},{6,4},{7,5},{8,10},{9,11},{10,... | collective-permute-start | bytes 786440 | tf_op jit(solution)/shard_map/ppermute | solution.py:48
  121.4 7.3 %collective-permute-done.7 = bf16[512,256]{0,1:T(8,128)(2,1)S(1)} collective-permute-done((bf16[512,256]{0,1:T(8,128)(2,1)S(1)}, bf16[512,256]{0,1:T(8,128)(2,1)S(1)}, u32[]{:S(2)}, u32[]{:S(2)}) %collective-permute-start.7) | collective-permute-done | bytes 262176 | tf_op jit(solution)/shard_map/ppermute | solution.py:48
  129.1 30.4 %all_to_all.25 = bf16[16,8,4,250]{3,2,1,0:T(4,128)(2,1)S(1)} all-to-all(bf16[16,8,4,250]{3,2,1,0:T(4,128)(2,1)S(1)} %reshape_reshape.10), channel_id=1, replica_groups=mesh['outer'=16,'inner'=8,'feat'=4] {'outer'}, dimensions={0} | all-to-all | bytes 512000 | tf_op jit(solution)/shard_map/all_to_all | solution.py:35
  160.3 4.1 %all-to-all-start.4 = ((bf16[8,16,4,250]{3,2,1,0:T(4,128)(2,1)}), bf16[8,16,4,250]{3,2,1,0:T(4,128)(2,1)S(1)}, u32[]{:S(2)}, u32[]{:S(2)}) async-start(bf16[8,16,4,250]{3,2,1,0:T(4,128)(2,1)} %copy.59), calls=%async_computation.4 | async-start | bytes 524288 | tf_op jit(solution)/shard_map/all_to_all | solution.py:35
  164.5 7.3 %all-to-all-done.4 = bf16[8,16,4,250]{3,2,1,0:T(4,128)(2,1)S(1)} async-done(((bf16[8,16,4,250]{3,2,1,0:T(4,128)(2,1)}), bf16[8,16,4,250]{3,2,1,0:T(4,128)(2,1)S(1)}, u32[]{:S(2)}, u32[]{:S(2)}) %all-to-all-start.4) | async-done | bytes 256032 | tf_op jit(solution)/shard_map/all_to_all | solution.py:35
  (73 shorter events, 26.1 us)
Async XLA Ops:
  0.0 32.4 %copy-start = (s32[128,7]{0,1:T(8,128)S(1)}, s32[128,7]{0,1:T(8,128)}, u32[]{:S(2)}) copy-start(s32[128,7]{0,1:T(8,128)} %param.8) | copy-start | bytes 10756
  0.0 23.7 %copy-start.4 = (s32[256,1]{0,1:T(1,128)S(1)}, s32[256,1]{0,1:T(1,128)}, u32[]{:S(2)}) copy-start(s32[256,1]{0,1:T(1,128)} %param.7) | copy-start | bytes 3076
  3.1 59.1 %collective-permute-start = (bf16[128,2048]{1,0:T(8,128)(2,1)S(1)}, bf16[128,2048]{1,0:T(8,128)(2,1)}, u32[]{:S(2)}, u32[]{:S(2)}) collective-permute-start(bf16[128,2048]{1,0:T(8,128)(2,1)S(1)} %concatenate.9), channel_id=1, source_target_pairs={{0,508},{4,0},{8,4},{12,8},{16,12},{20,16},{24,20},{28,24},{32,28}... | collective-permute-start | bytes 1572872 | tf_op jit(solution)/shard_map/ppermute | solution.py:43
  8.5 67.1 %collective-permute-start.1 = (bf16[128,2048]{1,0:T(8,128)(2,1)S(1)}, bf16[128,2048]{1,0:T(8,128)(2,1)S(1)}, u32[]{:S(2)}, u32[]{:S(2)}) collective-permute-start(bf16[128,2048]{1,0:T(8,128)(2,1)S(1)} %concatenate.9), channel_id=1, source_target_pairs={{0,4},{4,8},{8,12},{12,16},{16,20},{20,24},{24,28},{28,32},{32,36}... | collective-permute-start | bytes 1572872 | tf_op jit(solution)/shard_map/ppermute | solution.py:43
  10.4 66.0 %collective-permute-start.2 = (bf16[128,2048]{1,0:T(8,128)(2,1)S(1)}, bf16[128,2048]{1,0:T(8,128)(2,1)S(1)}, u32[]{:S(2)}, u32[]{:S(2)}) collective-permute-start(bf16[128,2048]{1,0:T(8,128)(2,1)S(1)} %concatenate.9), channel_id=1, source_target_pairs={{0,504},{4,508},{8,0},{12,4},{16,8},{20,12},{24,16},{28,20},{32,24... | collective-permute-start | bytes 1572872 | tf_op jit(solution)/shard_map/ppermute | solution.py:43
  13.4 63.8 %collective-permute-start.3 = (bf16[128,2048]{1,0:T(8,128)(2,1)S(1)}, bf16[128,2048]{1,0:T(8,128)(2,1)S(1)}, u32[]{:S(2)}, u32[]{:S(2)}) collective-permute-start(bf16[128,2048]{1,0:T(8,128)(2,1)S(1)} %concatenate.9), channel_id=1, source_target_pairs={{0,8},{4,12},{8,16},{12,20},{16,24},{20,28},{24,32},{28,36},{32,40... | collective-permute-start | bytes 1572872 | tf_op jit(solution)/shard_map/ppermute | solution.py:43
  16.3 69.7 %collective-permute-start.4 = (bf16[128,2048]{1,0:T(8,128)(2,1)S(1)}, bf16[128,2048]{1,0:T(8,128)(2,1)S(1)}, u32[]{:S(2)}, u32[]{:S(2)}) collective-permute-start(bf16[128,2048]{1,0:T(8,128)(2,1)S(1)} %concatenate.9), channel_id=1, source_target_pairs={{0,500},{4,504},{8,508},{12,0},{16,4},{20,8},{24,12},{28,16},{32,2... | collective-permute-start | bytes 1572872 | tf_op jit(solution)/shard_map/ppermute | solution.py:43
  26.7 19.7 %all-to-all-start = ((bf16[8,16,4,256]{3,2,1,0:T(4,128)(2,1)}), bf16[8,16,4,256]{3,2,1,0:T(4,128)(2,1)S(1)}, u32[]{:S(2)}, u32[]{:S(2)}) async-start(bf16[8,16,4,256]{3,2,1,0:T(4,128)(2,1)} %bitcast.83), calls=%async_computation | async-start | bytes 524288 | tf_op jit(solution)/shard_map/all_to_all | solution.py:35
  47.2 33.0 %all-to-all-start.1 = ((bf16[16,8,4,256]{3,2,1,0:T(4,128)(2,1)}), bf16[16,8,4,256]{3,2,1,0:T(4,128)(2,1)S(1)}, u32[]{:S(2)}, u32[]{:S(2)}) async-start(bf16[16,8,4,256]{3,2,1,0:T(4,128)(2,1)} %copy.53), calls=%async_computation.1 | async-start | bytes 524288 | tf_op jit(solution)/shard_map/all_to_all | solution.py:35
  62.1 32.7 %collective-permute-start.5 = (bf16[128,2048]{1,0:T(8,128)(2,1)S(1)}, bf16[128,2048]{1,0:T(8,128)(2,1)}, u32[]{:S(2)}, u32[]{:S(2)}) collective-permute-start(bf16[128,2048]{1,0:T(8,128)(2,1)S(1)} %concatenate.9), channel_id=1, source_target_pairs={{0,12},{4,16},{8,20},{12,24},{16,28},{20,32},{24,36},{28,40},{32,4... | collective-permute-start | bytes 1572872 | tf_op jit(solution)/shard_map/ppermute | solution.py:43
  81.5 23.4 %all-to-all-start.2 = ((bf16[4,512,256]{1,2,0:T(8,128)(2,1)}), bf16[4,512,256]{1,2,0:T(8,128)(2,1)S(1)}, u32[]{:S(2)}, u32[]{:S(2)}) async-start(bf16[4,512,256]{1,2,0:T(8,128)(2,1)} %stack.59), calls=%async_computation.2 | async-start | bytes 2097152 | tf_op jit(solution)/shard_map/all_to_all | solution.py:19
  96.7 2.6 %copy-start.1 = (bf16[7,128,2048]{2,1,0:T(8,128)(2,1)S(1)}, bf16[7,128,2048]{2,1,0:T(8,128)(2,1)}, u32[]{:S(2)}) copy-start(bf16[7,128,2048]{2,1,0:T(8,128)(2,1)} %bitcast_dynamic-update-slice_fusion) | copy-start | bytes 11010052
  107.8 1.5 copy-start.2
  110.7 1.3 copy-start.3
  112.7 3.8 %collective-permute-start.6 = (bf16[512,512]{0,1:T(8,128)(2,1)S(1)}, bf16[512,512]{0,1:T(8,128)(2,1)S(1)}, u32[]{:S(2)}, u32[]{:S(2)}) collective-permute-start(bf16[512,512]{0,1:T(8,128)(2,1)S(1)} %concatenate.10), channel_id=1, source_target_pairs={{0,1},{1,0},{2,3},{3,2},{4,5},{5,4},{6,7},{7,6},{8,9},{9,8},{10,11... | collective-permute-start | bytes 1572872 | tf_op jit(solution)/shard_map/ppermute | solution.py:48
  117.0 11.7 %collective-permute-start.7 = (bf16[512,256]{0,1:T(8,128)(2,1)S(1)}, bf16[512,256]{0,1:T(8,128)(2,1)S(1)}, u32[]{:S(2)}, u32[]{:S(2)}) collective-permute-start(bf16[512,256]{0,1:T(8,128)(2,1)S(1)} %concatenate.11), channel_id=1, source_target_pairs={{0,2},{1,3},{2,0},{3,1},{4,6},{5,7},{6,4},{7,5},{8,10},{9,11},{10,... | collective-permute-start | bytes 786440 | tf_op jit(solution)/shard_map/ppermute | solution.py:48
  160.3 11.4 %all-to-all-start.4 = ((bf16[8,16,4,250]{3,2,1,0:T(4,128)(2,1)}), bf16[8,16,4,250]{3,2,1,0:T(4,128)(2,1)S(1)}, u32[]{:S(2)}, u32[]{:S(2)}) async-start(bf16[8,16,4,250]{3,2,1,0:T(4,128)(2,1)} %copy.59), calls=%async_computation.4 | async-start | bytes 524288 | tf_op jit(solution)/shard_map/all_to_all | solution.py:35
